TPU v7x, 256 devices: a whole 4x4x8 slice. The times are simulated.
256 devices in a mesh: dp: 4 (over x_lo, core), expert: 64 (over z, y, x_hi).
Axes of the slice: x: 4 (x_hi: 2, x_lo: 2; x = x_hi * 2 + x_lo), y: 4, z: 8, core: 2. Of those that a mesh axis runs over, the one named last changes fastest.
Arguments:
- prev_acts: bfloat16 [4, 64, 128, 3584], P('dp', 'expert'), may hold values from -6 to 6
- prev_cot: bfloat16 [4, 64, 128, 512], P('dp', 'expert'), may hold values from -0.59765625 to 0.59765625
- weights: bfloat16 [64, 3584, 512], P('expert', 'dp'), may hold values from -0.09375 to 0.09375
- first_moment: float32 [64, 3584, 512], P('expert', 'dp'), may hold values from -1.8 to 1.8
- second_moment: float32 [64, 3584, 512], P('expert', 'dp'), may hold values from 0.1 to 2
- tokens: bfloat16 [4, 64, 128, 3584], P('dp', 'expert'), may hold values from -6 to 6
- routing: int32 [4, 64, 128, 2], P('dp', 'expert'), may hold values from 0 to 15, all different within a row; in each aligned block of 128 rows (0 to 127, 128 to 255, ..., all dimensions but the last counted through in order) at most 24 rows name the same one
- gates: bfloat16 [4, 64, 128, 2], P('dp', 'expert'), may hold values from 0.19921875 to 1
- token_counts: int32 [4, 64], P('dp', 'expert'), may hold values from 64 to 128
- old_owner: int32 [16], replicated, may hold values from 0 to 15, each once
- new_owner: int32 [16], replicated, may hold values from 0 to 15, each once
Outputs:
- expert_hidden: bfloat16 [4, 64, 1536, 256], P('dp', 'expert')
- new_weights: bfloat16 [64, 3584, 512], P('expert', 'dp')
- new_first: float32 [64, 3584, 512], P('expert', 'dp')
- new_second: float32 [64, 3584, 512], P('expert', 'dp')
Inputs may be any that keep to these rules, and one draw needn't show every extreme that they name: `routing`: each token names 2 different hot experts; within the rows of one device no hot expert is named by more than 24 rows. `old_owner`: each is a permutation of the 16 groups. `new_owner`: each is a permutation of the 16 groups.
All inputs are finite; a program needn't handle non-finite values.
Results may differ from a plain program's by a relative error of at most 0.013.
Values may be sent and summed in bfloat16 or wider, within the bound.
No kernel may reach another device: no remote copies, remote signals or barrier semaphores. Data moves between devices by JAX's collectives and lax.ppermute only.
A program may use at most 128 MiB of HBM per device.

v0:
```python
import jax
import jax.numpy as jnp
from jax import lax
from jax.sharding import Mesh
from jax.sharding import PartitionSpec as P

D = 3584
GRP = 4
SCALE_PAD = 128
beta_first = 0.9
beta_second = 0.95
learning = 0.00022
decay_rate = 0.1
epsilon = 1e-08
first_fix = 1.0 - 0.9**40
second_fix = 1.0 - 0.95**40


def adamw(weight_now, first_now, second_now, gradient):
    first_next = beta_first * first_now + (1.0 - beta_first) * gradient
    second_next = beta_second * second_now + (1.0 - beta_second) * gradient * gradient
    stepped = weight_now.astype(jnp.float32) * (1.0 - learning * decay_rate) - learning * (
        first_next / first_fix
    ) / (jnp.sqrt(second_next / second_fix) + epsilon)
    return (stepped.astype(jnp.bfloat16), first_next, second_next)


def migrate(state, group_source, groups, mode=None):
    layers, rows_dev, width = state.shape
    piece_rows = rows_dev // groups
    split = state.reshape(layers, groups, piece_rows, width)
    spread = lax.all_to_all(split, "grp", split_axis=1, concat_axis=1, tiled=True)
    chosen = jnp.take(spread, group_source, axis=1, mode=mode)
    home = lax.all_to_all(chosen, "grp", split_axis=1, concat_axis=1, tiled=True)
    return home.reshape(layers, rows_dev, width)


def pack_tokens(token_block, route_block, gate_block, limit, hot_index, capacity):
    valid = jnp.arange(token_block.shape[0], dtype=jnp.int32) < limit
    hits = (route_block[:, :, None] == hot_index[None, None, :]) & valid[:, None, None]
    named = jnp.sum(hits.astype(jnp.int32), axis=1)
    scales = jnp.sum(jnp.where(hits, gate_block.astype(jnp.float32)[:, :, None], 0.0), axis=1)
    ranks = jnp.cumsum(named, axis=0) - named
    slots = jnp.arange(capacity, dtype=jnp.int32)
    placed = (ranks.T[:, None, :] == slots[None, :, None]) & (named.T[:, None, :] == 1)
    packed = jnp.einsum(
        "hct,td->hcd", placed.astype(jnp.bfloat16), token_block, preferred_element_type=jnp.float32
    ).astype(jnp.bfloat16)
    gate_scale = jnp.einsum("hct,th->hc", placed.astype(jnp.float32), scales).astype(jnp.bfloat16)
    return (packed, gate_scale)


def local(
    prev_acts,
    prev_cot,
    weights,
    first_moment,
    second_moment,
    tokens,
    routing,
    gates,
    token_counts,
    old_owner,
    new_owner,
):
    groups = lax.axis_size("grp")
    experts = groups * GRP
    token_slots = tokens.shape[2]
    capacity = min(token_slots, 3 * token_slots // groups)
    width = weights.shape[2]
    hidden_units = width // 2
    activations = prev_acts[0, 0]
    cotangent = prev_cot[0, 0]
    hot_index = jnp.arange(groups, dtype=jnp.int32)
    holder = jnp.sum(
        jnp.where(new_owner[None, :] == hot_index[:, None], hot_index[None, :], 0), axis=1
    )
    group_source = jnp.take(old_owner, holder)
    packed, gate_scale = pack_tokens(
        tokens[0, 0], routing[0, 0], gates[0, 0], token_counts[0, 0], holder, capacity
    )
    scale_cols = jnp.zeros((groups, capacity, SCALE_PAD), jnp.bfloat16).at[:, :, 0].set(gate_scale)
    payload = jnp.concatenate([packed, scale_cols], axis=2)
    by_group = lax.all_to_all(payload, "grp", split_axis=0, concat_axis=0, tiled=True)
    grads = lax.psum_scatter(
        lax.dot_general(
            activations, cotangent, (((0,), (0,)), ((), ())), preferred_element_type=jnp.float32
        ).astype(jnp.bfloat16),
        "dp",
        scatter_dimension=0,
        tiled=True,
    )
    by_group, grads = lax.optimization_barrier((by_group, grads))
    grads = grads.astype(jnp.float32)
    near = lax.all_gather(by_group, "ylo", axis=0, tiled=False)
    near = near.reshape(2 * groups * capacity, D + SCALE_PAD)
    stepped, first_next, second_next = adamw(weights[0], first_moment[0], second_moment[0], grads)
    weight_home = migrate(stepped[None], group_source, groups)
    new_weight = weight_home[0]
    moments = jnp.stack([first_next.astype(jnp.bfloat16), second_next.astype(jnp.bfloat16)])
    moments, new_weight = lax.optimization_barrier((moments, new_weight))
    moved = migrate(moments, group_source, groups, mode="clip")
    both = lax.all_gather(new_weight, ("xhi", "dp"), axis=0, tiled=True)
    both = both.reshape(2, -1, width)
    both = jnp.pad(both, ((0, 0), (0, SCALE_PAD), (0, 0)))
    projected = jnp.stack(
        [jnp.dot(near, both[k], preferred_element_type=jnp.float32) for k in range(2)]
    )
    scaling = near[:, D].astype(jnp.float32)
    result = (
        jax.nn.silu(projected[:, :, :hidden_units])
        * projected[:, :, hidden_units:]
        * scaling[None, :, None]
    ).astype(jnp.bfloat16)
    xhi = lax.axis_index("xhi")
    own = lax.dynamic_index_in_dim(result, xhi, axis=0, keepdims=False)
    other = lax.dynamic_index_in_dim(result, 1 - xhi, axis=0, keepdims=False)
    for_partner = lax.ppermute(other, "xhi", perm=[(0, 1), (1, 0)])
    mine = jnp.where(
        xhi == 0, jnp.stack([own, for_partner]), jnp.stack([for_partner, own])
    ).reshape(2, 2, groups, capacity, hidden_units)
    hidden = jnp.transpose(mine, (2, 1, 0, 3, 4)).reshape(1, 1, experts * capacity, hidden_units)
    return (
        hidden,
        weight_home,
        moved[0].astype(jnp.float32)[None],
        moved[1].astype(jnp.float32)[None],
    )


def solution(mesh):
    n_dp = mesh.shape["dp"]
    n_expert = mesh.shape["expert"]
    mesh4 = Mesh(mesh.devices.reshape(n_dp, n_expert // GRP, 2, 2), ("dp", "grp", "ylo", "xhi"))
    ex = ("grp", "ylo", "xhi")
    in_specs = (
        P("dp", ex, None, None),
        P("dp", ex, None, None),
        P(ex, "dp", None),
        P(ex, "dp", None),
        P(ex, "dp", None),
        P("dp", ex, None, None),
        P("dp", ex, None, None),
        P("dp", ex, None, None),
        P("dp", ex),
        P(),
        P(),
    )
    out_specs = (P("dp", ex, None, None), P(ex, "dp", None), P(ex, "dp", None), P(ex, "dp", None))
    return jax.shard_map(local, mesh=mesh4, in_specs=in_specs, out_specs=out_specs, check_vma=False)
```

profile of v0, /device:TPU:6, one launch (start us, length us, event | category | flops | bytes accessed | tf_op | source)
XLA Modules:
  0.0 284.6 jit_solution(10818399610023016619)
XLA Ops:
  7.2 0.0 copy-start
  7.2 0.0 reduce-scatter.2.cloned.1.call-start
  7.2 1.1 copy-done
  8.3 3.8 %convolution_convert_fusion = bf16[3584,512]{1,0:T(8,128)(2,1)} fusion(bf16[1,1,128,3584]{3,2,1,0:T(8,128)(2,1)S(1)} %copy-done, bf16[1,1,128,512]{3,2,1,0:T(8,128)(2,1)} %param.14), kind=kOutput, calls=%fused_computation.5 | convolution fusion | flops 471597056 | bytes 4718592 | tf_op jit(solution)/shard_map/dot_general | solution.py:86
  12.2 0.0 copy-start.9
  12.2 0.0 copy-start.7
  12.2 0.0 copy-start.10
  12.2 0.0 reduce-scatter.2.cloned.1.call-update
  12.2 0.0 all-gather.6.cloned.1.call-start
  12.3 0.6 copy-done.9
  12.8 0.1 select_reduce_fusion.1
  13.6 0.0 copy-done.7
  13.6 0.1 convert_reduce_fusion
  13.7 0.1 copy.42
  13.8 0.2 reduce_window_sum.11
  14.0 0.1 copy.44
  14.1 0.0 copy-done.10
  14.1 0.1 select_reduce_fusion
  14.2 0.2 fusion.30
  14.3 0.2 copy.45
  14.5 0.0 copy-done.4
  14.5 0.9 convolution_convert_fusion.1
  15.4 0.2 fusion.7
  15.6 80.3 %all_to_all.25 = bf16[16,24,3712]{2,1,0:T(8,128)(2,1)} all-to-all(bf16[16,24,3712]{2,1,0:T(8,128)(2,1)S(1)} %fusion.7), channel_id=1, replica_groups=mesh['dp'=4,'grp'=16,'ylo'=2,'xhi'=2] {'grp'}, dimensions={0} | all-to-all | bytes 5701632 | tf_op jit(solution)/shard_map/all_to_all | solution.py:84
  95.9 0.0 all-gather.6.cloned.1.call-update
  96.0 1.1 copy-done.5
  97.1 5.1 %fusion.10 = (bf16[896,512]{1,0:T(8,128)(2,1)}, bf16[1,896,512]{2,1,0:T(8,128)(2,1)S(1)}, bf16[1,896,512]{2,1,0:T(8,128)(2,1)}) fusion(bf16[1,896,512]{2,1,0:T(8,128)(2,1)S(1)} %copy-done.5, bf16[896,512]{1,0:T(8,128)(2,1)} %reduce-scatter.2.cloned.1.call-done, f32[1,896,512]{2,1,0:T(8,128)} %param.16, f32[1,896,512]{2,1,0:T(8,128)} %param.17), kind=kLoop, calls=%fused_computation.22 | loop fusion | flops 8257536 | bytes 8257536 | tf_op jit(solution)/shard_map/convert_element_type | solution.py:25
  102.3 3.8 %all-to-all-start.1 = ((bf16[1,16,56,512]{3,2,0,1:T(8,128)(2,1)}), bf16[1,16,56,512]{3,2,0,1:T(8,128)(2,1)S(1)}, u32[]{:S(2)}, u32[]{:S(2)}) async-start(bf16[1,16,56,512]{3,2,0,1:T(8,128)(2,1)} %bitcast.125), calls=%async_computation.2 | async-start | bytes 1835008 | tf_op jit(solution)/shard_map/all_to_all | solution.py:32
  106.1 0.0 copy-done.1
  106.1 0.7 gather_fusion
  106.8 24.6 %all-to-all-done.1 = bf16[1,16,56,512]{3,2,0,1:T(8,128)(2,1)S(1)} async-done(((bf16[1,16,56,512]{3,2,0,1:T(8,128)(2,1)}), bf16[1,16,56,512]{3,2,0,1:T(8,128)(2,1)S(1)}, u32[]{:S(2)}, u32[]{:S(2)}) %all-to-all-start.1) | async-done | bytes 917536 | tf_op jit(solution)/shard_map/all_to_all | solution.py:32
  131.4 1.5 gather_fusion.1
  132.9 2.2 fusion.26
  135.2 3.8 %all-to-all-start.2 = ((bf16[1,16,56,512]{3,2,0,1:T(8,128)(2,1)}), bf16[1,16,56,512]{3,2,0,1:T(8,128)(2,1)S(1)}, u32[]{:S(2)}, u32[]{:S(2)}) async-start(bf16[1,16,56,512]{3,2,0,1:T(8,128)(2,1)} %fusion.26), calls=%async_computation.3 | async-start | bytes 1835008 | tf_op jit(solution)/shard_map/all_to_all | solution.py:34
  139.0 0.0 all-gather.4.cloned.1.call-start
  139.0 2.6 pad_maximum_fusion
  141.6 24.7 %all-to-all-done.2 = bf16[1,16,56,512]{3,2,0,1:T(8,128)(2,1)S(1)} async-done(((bf16[1,16,56,512]{3,2,0,1:T(8,128)(2,1)}), bf16[1,16,56,512]{3,2,0,1:T(8,128)(2,1)S(1)}, u32[]{:S(2)}, u32[]{:S(2)}) %all-to-all-start.2) | async-done | bytes 917536 | tf_op jit(solution)/shard_map/all_to_all | solution.py:34
  166.4 0.9 copy-done.2
  167.3 0.0 all-gather.4.cloned.1.call-update
  167.3 3.0 %copy.50 = bf16[2,16,56,512]{3,2,0,1:T(8,128)(2,1)} copy(bf16[2,16,56,512]{3,2,1,0:T(8,128)(2,1)} %bitcast.120) | data formatting | bytes 3670016 | tf_op jit(solution)/shard_map/reshape | solution.py:31
  170.3 3.7 %all-to-all-start.3 = ((bf16[2,16,56,512]{3,2,0,1:T(8,128)(2,1)}), bf16[2,16,56,512]{3,2,0,1:T(8,128)(2,1)S(1)}, u32[]{:S(2)}, u32[]{:S(2)}) async-start(bf16[2,16,56,512]{3,2,0,1:T(8,128)(2,1)} %copy.50), calls=%async_computation.4 | async-start | bytes 3670016 | tf_op jit(solution)/shard_map/all_to_all | solution.py:32
  174.0 45.9 %all-to-all-done.3 = bf16[2,16,56,512]{3,2,0,1:T(8,128)(2,1)S(1)} async-done(((bf16[2,16,56,512]{3,2,0,1:T(8,128)(2,1)}), bf16[2,16,56,512]{3,2,0,1:T(8,128)(2,1)S(1)}, u32[]{:S(2)}, u32[]{:S(2)}) %all-to-all-start.3) | async-done | bytes 1835040 | tf_op jit(solution)/shard_map/all_to_all | solution.py:32
  219.9 1.9 gather_fusion.2
  221.7 3.7 %all-to-all-start.4 = ((bf16[2,16,56,512]{3,2,0,1:T(8,128)(2,1)}), bf16[2,16,56,512]{3,2,0,1:T(8,128)(2,1)S(1)}, u32[]{:S(2)}, u32[]{:S(2)}) async-start(bf16[2,16,56,512]{3,2,0,1:T(8,128)(2,1)} %bitcast.121), calls=%async_computation.5 | async-start | bytes 3670016 | tf_op jit(solution)/shard_map/all_to_all | solution.py:34
  225.5 0.0 all-gather.6.cloned.1.call-done
  225.5 0.9 slice.57
  226.5 0.1 copy.53
  226.6 14.0 %all-gather.4.cloned.1.call-done = bf16[7168,512]{1,0:T(8,128)(2,1)} async-done(((bf16[896,512]{1,0:T(8,128)(2,1)}), bf16[7168,512]{1,0:T(8,128)(2,1)}) %all-gather.4.cloned.1.call-update) | async-done | bytes 7340048 | tf_op jit(solution)/shard_map/all_gather | solution.py:103
  240.6 6.3 %fusion.15 = f32[1,768,512]{2,1,0:T(8,128)S(1)} fusion(bf16[768,3712]{1,0:T(8,128)(2,1)} %bitcast.131, bf16[2,3584,512]{2,1,0:T(8,128)(2,1)} %bitcast.135), kind=kOutput, calls=%fused_computation.28 | convolution fusion | flops 2919235584 | bytes 14614528 | tf_op jit(solution)/shard_map/dot_general | solution.py:107
  246.9 0.0 copy-done.6
  247.0 1.2 copy-done.8
  248.1 3.1 %fusion.18 = f32[1,768,512]{2,1,0:T(8,128)S(1)} fusion(bf16[768,3712]{1,0:T(8,128)(2,1)S(1)} %bitcast.132, bf16[2,3584,512]{2,1,0:T(8,128)(2,1)S(1)} %bitcast.136), kind=kOutput, calls=%fused_computation.29 | convolution fusion | flops 2919235584 | bytes 14614528 | tf_op jit(solution)/shard_map/dot_general | solution.py:107
  251.2 0.4 fusion.14
  251.6 0.1 constant_dynamic-slice_fusion
  251.7 2.5 collective-permute-start
  254.3 17.5 %all-to-all-done.4 = bf16[2,16,56,512]{3,2,0,1:T(8,128)(2,1)S(1)} async-done(((bf16[2,16,56,512]{3,2,0,1:T(8,128)(2,1)}), bf16[2,16,56,512]{3,2,0,1:T(8,128)(2,1)S(1)}, u32[]{:S(2)}, u32[]{:S(2)}) %all-to-all-start.4) | async-done | bytes 1835040 | tf_op jit(solution)/shard_map/all_to_all | solution.py:34
  271.8 0.1 fusion.43
  271.9 1.5 convert.5
  273.4 1.5 convert.6
  274.8 0.0 collective-permute-done
  274.9 1.3 fusion.28
  276.2 1.0 copy.49
  277.1 0.0 copy-done.3
  277.1 0.9 copy.56
  (20 shorter events, 0.1 us)
Async XLA Ops:
  7.2 1.2 copy-start
  7.2 88.7 %reduce-scatter.2.cloned.1.call-start = ((), (), s32[]{:S(2)}) async-start(), calls=%async_computation.6 | async-start | bytes 4587520 | tf_op jit(solution)/shard_map/reduce_scatter | solution.py:85
  12.2 0.7 copy-start.9
  12.2 1.4 copy-start.7
  12.2 1.9 copy-start.10
  12.2 2.3 copy-start.4
  12.2 213.3 %all-gather.6.cloned.1.call-start = ((), (), s32[]{:S(2)}) async-start(), calls=%async_computation.8 | async-start | bytes 8552448 | tf_op jit(solution)/shard_map/all_gather | solution.py:95
  95.9 1.2 copy-start.5
  102.2 3.8 %copy-start.1 = (s32[16]{0:T(128)S(1)}, s32[16]{0:T(128)}, u32[]{:S(2)}) copy-start(s32[16]{0:T(128)} %param.22) | copy-start | bytes 196
  102.3 29.1 %all-to-all-start.1 = ((bf16[1,16,56,512]{3,2,0,1:T(8,128)(2,1)}), bf16[1,16,56,512]{3,2,0,1:T(8,128)(2,1)S(1)}, u32[]{:S(2)}, u32[]{:S(2)}) async-start(bf16[1,16,56,512]{3,2,0,1:T(8,128)(2,1)} %bitcast.125), calls=%async_computation.2 | async-start | bytes 1835008 | tf_op jit(solution)/shard_map/all_to_all | solution.py:32
  135.2 31.2 %all-to-all-start.2 = ((bf16[1,16,56,512]{3,2,0,1:T(8,128)(2,1)}), bf16[1,16,56,512]{3,2,0,1:T(8,128)(2,1)S(1)}, u32[]{:S(2)}, u32[]{:S(2)}) async-start(bf16[1,16,56,512]{3,2,0,1:T(8,128)(2,1)} %fusion.26), calls=%async_computation.3 | async-start | bytes 1835008 | tf_op jit(solution)/shard_map/all_to_all | solution.py:34
  139.0 101.6 %all-gather.4.cloned.1.call-start = ((), (), s32[]{:S(2)}) async-start(), calls=%async_computation.7 | async-start | bytes 8257536 | tf_op jit(solution)/shard_map/all_gather | solution.py:103
  166.4 0.9 copy-start.2
  170.3 49.6 %all-to-all-start.3 = ((bf16[2,16,56,512]{3,2,0,1:T(8,128)(2,1)}), bf16[2,16,56,512]{3,2,0,1:T(8,128)(2,1)S(1)}, u32[]{:S(2)}, u32[]{:S(2)}) async-start(bf16[2,16,56,512]{3,2,0,1:T(8,128)(2,1)} %copy.50), calls=%async_computation.4 | async-start | bytes 3670016 | tf_op jit(solution)/shard_map/all_to_all | solution.py:32
  221.7 50.0 %all-to-all-start.4 = ((bf16[2,16,56,512]{3,2,0,1:T(8,128)(2,1)}), bf16[2,16,56,512]{3,2,0,1:T(8,128)(2,1)S(1)}, u32[]{:S(2)}, u32[]{:S(2)}) async-start(bf16[2,16,56,512]{3,2,0,1:T(8,128)(2,1)} %bitcast.121), calls=%async_computation.5 | async-start | bytes 3670016 | tf_op jit(solution)/shard_map/all_to_all | solution.py:34
  240.6 6.3 %copy-start.6 = (bf16[32,24,3712]{2,1,0:T(8,128)(2,1)S(1)}, bf16[32,24,3712]{2,1,0:T(8,128)(2,1)}, u32[]{:S(2)}) copy-start(bf16[32,24,3712]{2,1,0:T(8,128)(2,1)} %all-gather.6.cloned.1.call-done) | copy-start | bytes 17104900
  240.6 7.5 %copy-start.8 = (bf16[7168,512]{1,0:T(8,128)(2,1)S(1)}, bf16[7168,512]{1,0:T(8,128)(2,1)}, u32[]{:S(2)}) copy-start(bf16[7168,512]{1,0:T(8,128)(2,1)} %all-gather.4.cloned.1.call-done) | copy-start | bytes 22020100
  251.7 23.1 %collective-permute-start = (bf16[768,256]{1,0:T(8,128)(2,1)S(1)}, bf16[768,256]{1,0:T(8,128)(2,1)}, u32[]{:S(2)}, u32[]{:S(2)}) collective-permute-start(bf16[768,256]{1,0:T(8,128)(2,1)S(1)} %get-tuple-element.30), channel_id=1, source_target_pairs={{0,1},{1,0},{2,3},{3,2},{4,5},{5,4},{6,7},{7,6},{8,9},{9,8},{10,11... | collective-permute-start | bytes 1179656 | tf_op jit(solution)/shard_map/ppermute | solution.py:118
  274.8 2.3 copy-start.3
Sparse Core Ops, SparseCore 0:
  12.3 45.8 reduce-scatter.1
  96.1 95.5 all-gather.5
  194.1 46.5 all-gather.3
where the time goes:
time: 285 us
  waiting for transfers between devices  127 us (45%)
  blocking collectives  80.3 us (28%)
  starting transfers between devices  17.7 us (6%)
  local copies, waits for them, and re-layouts  15.5 us (5%)
  other arithmetic  15.4 us (5%)
  between operations  14.6 us (5%)
  matrix products  14.2 us (5%)
    all_to_all x1, blocking collectives, local(): lax.all_to_all(payload, 'grp', split_axis=0, concat_axis=0, tiled=True)  80.3 us
    all_to_all x2, waiting for transfers between devices, migrate(): lax.all_to_all(split, 'grp', split_axis=1, concat_axis=1, tiled=True)  70.5 us
    all_to_all x2, waiting for transfers between devices, migrate(): lax.all_to_all(chosen, 'grp', split_axis=1, concat_axis=1, tiled=True)  42.2 us
    all_gather x1, waiting for transfers between devices, local(): both = lax.all_gather(new_weight, ('xhi', 'dp'), axis=0, tiled=True)  14 us
    dot_general x2, matrix products, local(): jnp.dot(near, both[k], preferred_element_type=jnp.float32)  9.38 us
    all_to_all x2, starting transfers between devices, migrate(): lax.all_to_all(chosen, 'grp', split_axis=1, concat_axis=1, tiled=True)  7.54 us
    all_to_all x2, starting transfers between devices, migrate(): lax.all_to_all(split, 'grp', split_axis=1, concat_axis=1, tiled=True)  7.49 us
    unnamed x24, local copies, waits for them, and re-layouts  6 us
  transfers between devices with their start and end apart: 8, of which 5 were waited for; matrix products, arithmetic and copies ran while one was open for 12% of the time, Pallas kernels for 0%

commit v1 on v0

--- a/solution.py
+++ b/solution.py
@@ -100,7 +100,10 @@
     moments = jnp.stack([first_next.astype(jnp.bfloat16), second_next.astype(jnp.bfloat16)])
     moments, new_weight = lax.optimization_barrier((moments, new_weight))
     moved = migrate(moments, group_source, groups, mode="clip")
-    both = lax.all_gather(new_weight, ("xhi", "dp"), axis=0, tiled=True)
+    both = jnp.concatenate(
+        lax.all_to_all(jnp.stack([new_weight] * lax.axis_size(("xhi", "dp"))), ("xhi", "dp"), 0, 0),
+        axis=0,
+    )
     both = both.reshape(2, -1, width)
     both = jnp.pad(both, ((0, 0), (0, SCALE_PAD), (0, 0)))
     projected = jnp.stack(

time: 285 us -> 373 us (1.31)
  blocking collectives: 80.3 us -> 131 us
  waiting for transfers between devices: 127 us -> 159 us
    all_to_all x0 -> x1, waiting for transfers between devices: none -> 77.2 us  [local(): lax.all_to_all(jnp.stack([new_weight] * lax.axis_size(('xhi', 'dp'))), ('...]
    all_to_all x0 -> x1, blocking collectives: none -> 50.2 us  [migrate(): lax.all_to_all(split, 'grp', split_axis=1, concat_axis=1, tiled=True)]
    all_to_all x2 -> x1, waiting for transfers between devices: 70.5 us -> 24.6 us  [migrate(): lax.all_to_all(split, 'grp', split_axis=1, concat_axis=1, tiled=True)]
    all_gather x1 -> x0, waiting for transfers between devices: 14 us -> none  [local(): both = lax.all_gather(new_weight, ('xhi', 'dp'), axis=0, tiled=True)]
    ppermute x1, waiting for transfers between devices: 0.01 us -> 10.1 us  [local(): for_partner = lax.ppermute(other, 'xhi', perm=[(0, 1), (1, 0)])]
    all_to_all x0 -> x1, starting transfers between devices: none -> 5.23 us  [local(): lax.all_to_all(jnp.stack([new_weight] * lax.axis_size(('xhi', 'dp'))), ('...]
    all_to_all x2, waiting for transfers between devices: 42.2 us -> 46.4 us  [migrate(): lax.all_to_all(chosen, 'grp', split_axis=1, concat_axis=1, tiled=True)]
    all_to_all x2 -> x1, starting transfers between devices: 7.49 us -> 3.77 us  [migrate(): lax.all_to_all(split, 'grp', split_axis=1, concat_axis=1, tiled=True)]
  transfers between devices with their start and end apart: 8 -> 7, of which waited for: 5 -> 5; matrix products, arithmetic and copies ran while one was open for 12% -> 6% of each run, Pallas kernels for 0% -> 0%
where the time goes in v1:
time: 373 us; the launch traced here: 371 us
  waiting for transfers between devices  159 us (43%)
  blocking collectives  131 us (35%)
  starting transfers between devices  19.4 us (5%)
  local copies, waits for them, and re-layouts  17.7 us (5%)
  matrix products  16.3 us (4%)
  between operations  14.9 us (4%)
  other arithmetic  13.2 us (4%)
    all_to_all x1, blocking collectives, local(): lax.all_to_all(payload, 'grp', split_axis=0, concat_axis=0, tiled=True)  80.4 us
    all_to_all x1, waiting for transfers between devices, local(): lax.all_to_all(jnp.stack([new_weight] * lax.axis_size(('xhi', 'dp'))), ('...  77.2 us
    all_to_all x1, blocking collectives, migrate(): lax.all_to_all(split, 'grp', split_axis=1, concat_axis=1, tiled=True)  50.2 us
    all_to_all x2, waiting for transfers between devices, migrate(): lax.all_to_all(chosen, 'grp', split_axis=1, concat_axis=1, tiled=True)  46.4 us
    all_to_all x1, waiting for transfers between devices, migrate(): lax.all_to_all(split, 'grp', split_axis=1, concat_axis=1, tiled=True)  24.6 us
    dot_general x2, matrix products, local(): jnp.dot(near, both[k], preferred_element_type=jnp.float32)  11.4 us
    ppermute x1, waiting for transfers between devices, local(): for_partner = lax.ppermute(other, 'xhi', perm=[(0, 1), (1, 0)])  10.1 us
    all_to_all x2, starting transfers between devices, migrate(): lax.all_to_all(chosen, 'grp', split_axis=1, concat_axis=1, tiled=True)  8.17 us
  transfers between devices with their start and end apart: 7, of which 5 were waited for; matrix products, arithmetic and copies ran while one was open for 6% of the time, Pallas kernels for 0%

profile of v1, /device:TPU:6, one launch (start us, length us, event | category | flops | bytes accessed | tf_op | source)
XLA Modules:
  0.0 371.2 jit_solution(12327504678911778900)
XLA Ops:
  7.2 0.0 copy-start
  7.2 0.0 reduce-scatter.2.cloned.1.call-start
  7.2 1.1 copy-done
  8.4 3.8 %convolution_convert_fusion = bf16[3584,512]{1,0:T(8,128)(2,1)} fusion(bf16[1,1,128,3584]{3,2,1,0:T(8,128)(2,1)S(1)} %copy-done, bf16[1,1,128,512]{3,2,1,0:T(8,128)(2,1)} %param.14), kind=kOutput, calls=%fused_computation.5 | convolution fusion | flops 471597056 | bytes 4718592 | tf_op jit(solution)/shard_map/dot_general | solution.py:86
  12.2 0.0 copy-start.8
  12.2 0.0 copy-start.7
  12.2 0.0 copy-start.9
  12.2 0.0 reduce-scatter.2.cloned.1.call-update
  12.2 0.6 copy-done.8
  12.8 0.1 select_reduce_fusion.1
  13.6 0.0 copy-done.7
  13.6 0.1 convert_reduce_fusion
  13.7 0.1 copy.42
  13.8 0.2 reduce_window_sum.11
  14.0 0.1 copy.44
  14.1 0.0 copy-done.9
  14.1 0.1 select_reduce_fusion
  14.2 0.2 fusion.30
  14.3 0.2 copy.45
  14.5 0.0 copy-done.4
  14.5 0.9 convolution_convert_fusion.1
  15.4 0.2 fusion.7
  15.6 0.0 copy-start.5
  15.6 80.4 %all_to_all.30 = bf16[16,24,3712]{2,1,0:T(8,128)(2,1)} all-to-all(bf16[16,24,3712]{2,1,0:T(8,128)(2,1)S(1)} %fusion.7), channel_id=1, replica_groups=mesh['dp'=4,'grp'=16,'ylo'=2,'xhi'=2] {'grp'}, dimensions={0} | all-to-all | bytes 5701632 | tf_op jit(solution)/shard_map/all_to_all | solution.py:84
  96.1 0.0 copy-done.5
  96.1 5.1 %fusion.10 = (bf16[896,512]{1,0:T(8,128)(2,1)}, bf16[1,896,512]{2,1,0:T(8,128)(2,1)S(1)}, bf16[1,896,512]{2,1,0:T(8,128)(2,1)}) fusion(bf16[1,896,512]{2,1,0:T(8,128)(2,1)S(1)} %copy-done.5, bf16[896,512]{1,0:T(8,128)(2,1)} %reduce-scatter.2.cloned.1.call-done, f32[1,896,512]{2,1,0:T(8,128)} %param.16, f32[1,896,512]{2,1,0:T(8,128)} %param.17), kind=kLoop, calls=%fused_computation.22 | loop fusion | flops 8257536 | bytes 8257536 | tf_op jit(solution)/shard_map/convert_element_type | solution.py:25
  101.2 3.8 %all-to-all-start.1 = ((bf16[1,16,56,512]{3,2,0,1:T(8,128)(2,1)}), bf16[1,16,56,512]{3,2,0,1:T(8,128)(2,1)S(1)}, u32[]{:S(2)}, u32[]{:S(2)}) async-start(bf16[1,16,56,512]{3,2,0,1:T(8,128)(2,1)} %bitcast.125), calls=%async_computation.2 | async-start | bytes 1835008 | tf_op jit(solution)/shard_map/all_to_all | solution.py:32
  105.0 0.0 copy-done.2
  105.0 0.7 gather_fusion
  105.7 24.6 %all-to-all-done.1 = bf16[1,16,56,512]{3,2,0,1:T(8,128)(2,1)S(1)} async-done(((bf16[1,16,56,512]{3,2,0,1:T(8,128)(2,1)}), bf16[1,16,56,512]{3,2,0,1:T(8,128)(2,1)S(1)}, u32[]{:S(2)}, u32[]{:S(2)}) %all-to-all-start.1) | async-done | bytes 917536 | tf_op jit(solution)/shard_map/all_to_all | solution.py:32
  130.4 1.5 gather_fusion.1
  131.9 2.3 fusion.26
  134.2 3.8 %all-to-all-start.2 = ((bf16[1,16,56,512]{3,2,0,1:T(8,128)(2,1)}), bf16[1,16,56,512]{3,2,0,1:T(8,128)(2,1)S(1)}, u32[]{:S(2)}, u32[]{:S(2)}) async-start(bf16[1,16,56,512]{3,2,0,1:T(8,128)(2,1)} %fusion.26), calls=%async_computation.3 | async-start | bytes 1835008 | tf_op jit(solution)/shard_map/all_to_all | solution.py:34
  138.0 0.0 copy-done.3
  138.0 1.4 pad_maximum_fusion
  139.4 26.2 %all-to-all-done.2 = bf16[1,16,56,512]{3,2,0,1:T(8,128)(2,1)S(1)} async-done(((bf16[1,16,56,512]{3,2,0,1:T(8,128)(2,1)}), bf16[1,16,56,512]{3,2,0,1:T(8,128)(2,1)S(1)}, u32[]{:S(2)}, u32[]{:S(2)}) %all-to-all-start.2) | async-done | bytes 917536 | tf_op jit(solution)/shard_map/all_to_all | solution.py:34
  165.5 1.7 copy.50
  167.3 50.2 %all_to_all.31 = bf16[2,16,56,512]{3,2,0,1:T(8,128)(2,1)} all-to-all(bf16[2,16,56,512]{3,2,0,1:T(8,128)(2,1)S(1)} %copy.50), channel_id=1, replica_groups=mesh['dp'=4,'grp'=16,'ylo'=2,'xhi'=2] {'grp'}, dimensions={1} | all-to-all | bytes 3670016 | tf_op jit(solution)/shard_map/all_to_all | solution.py:32
  217.4 3.6 stack.46
  221.1 5.2 %all-to-all-start.3 = ((bf16[8,896,512]{2,1,0:T(8,128)(2,1)}), bf16[8,896,512]{2,1,0:T(8,128)(2,1)}, u32[]{:S(2)}, u32[]{:S(2)}) async-start(bf16[8,896,512]{2,1,0:T(8,128)(2,1)} %stack.46), calls=%async_computation.4 | async-start | bytes 14680064 | tf_op jit(solution)/shard_map/all_to_all | solution.py:104
  226.3 0.0 all-gather.3.cloned.1.call-start
  226.3 0.7 all-gather.3.cloned.1.call-update
  227.1 3.4 gather_fusion.2
  230.5 77.2 %all-to-all-done.3 = bf16[8,896,512]{2,1,0:T(8,128)(2,1)} async-done(((bf16[8,896,512]{2,1,0:T(8,128)(2,1)}), bf16[8,896,512]{2,1,0:T(8,128)(2,1)}, u32[]{:S(2)}, u32[]{:S(2)}) %all-to-all-start.3) | async-done | bytes 7340064 | tf_op jit(solution)/shard_map/all_to_all | solution.py:104
  307.7 4.4 %all-to-all-start.5 = ((bf16[2,16,56,512]{3,2,0,1:T(8,128)(2,1)}), bf16[2,16,56,512]{3,2,0,1:T(8,128)(2,1)}, u32[]{:S(2)}, u32[]{:S(2)}) async-start(bf16[2,16,56,512]{3,2,0,1:T(8,128)(2,1)} %bitcast.121), calls=%async_computation.6 | async-start | bytes 3670016 | tf_op jit(solution)/shard_map/all_to_all | solution.py:34
  312.1 0.0 all-gather.3.cloned.1.call-done
  312.2 0.9 slice.57
  313.1 0.1 copy.53
  313.3 0.0 copy-start.6
  313.3 6.3 %fusion.18 = f32[1,768,512]{2,1,0:T(8,128)S(1)} fusion(bf16[768,3712]{1,0:T(8,128)(2,1)} %bitcast.132, bf16[2,3584,512]{2,1,0:T(8,128)(2,1)} %bitcast.30), kind=kOutput, calls=%fused_computation.29 | convolution fusion | flops 2919235584 | bytes 14614528 | tf_op jit(solution)/shard_map/dot_general | solution.py:110
  319.6 0.0 copy-done.6
  319.6 5.1 %fusion.15 = f32[1,768,512]{2,1,0:T(8,128)S(1)} fusion(bf16[768,3712]{1,0:T(8,128)(2,1)S(1)} %bitcast.133, bf16[2,3584,512]{2,1,0:T(8,128)(2,1)} %bitcast.30), kind=kOutput, calls=%fused_computation.28 | convolution fusion | flops 2919235584 | bytes 14614528 | tf_op jit(solution)/shard_map/dot_general | solution.py:110
  324.7 0.4 fusion.14
  325.2 0.1 constant_dynamic-slice_fusion
  325.3 2.2 collective-permute-start
  327.4 10.1 %collective-permute-done = bf16[768,256]{1,0:T(8,128)(2,1)S(1)} collective-permute-done((bf16[768,256]{1,0:T(8,128)(2,1)S(1)}, bf16[768,256]{1,0:T(8,128)(2,1)S(1)}, u32[]{:S(2)}, u32[]{:S(2)}) %collective-permute-start) | collective-permute-done | bytes 393248 | tf_op jit(solution)/shard_map/ppermute | solution.py:121
  337.5 0.1 fusion.28
  337.6 1.0 copy.49
  338.6 20.3 %all-to-all-done.5 = bf16[2,16,56,512]{3,2,0,1:T(8,128)(2,1)} async-done(((bf16[2,16,56,512]{3,2,0,1:T(8,128)(2,1)}), bf16[2,16,56,512]{3,2,0,1:T(8,128)(2,1)}, u32[]{:S(2)}, u32[]{:S(2)}) %all-to-all-start.5) | async-done | bytes 1835040 | tf_op jit(solution)/shard_map/all_to_all | solution.py:34
  358.9 1.6 fusion.43
  360.5 1.5 convert.5
  361.9 1.5 convert.6
  363.4 0.9 copy.56
  364.3 0.0 copy-done.1
  (17 shorter events, 0.1 us)
Async XLA Ops:
  7.2 1.2 copy-start
  7.2 88.9 %reduce-scatter.2.cloned.1.call-start = ((), (), s32[]{:S(2)}) async-start(), calls=%async_computation.7 | async-start | bytes 4587520 | tf_op jit(solution)/shard_map/reduce_scatter | solution.py:85
  12.2 0.7 copy-start.8
  12.2 1.4 copy-start.7
  12.2 1.9 copy-start.9
  12.2 2.3 copy-start.4
  15.6 80.5 %copy-start.5 = (bf16[1,896,512]{2,1,0:T(8,128)(2,1)S(1)}, bf16[1,896,512]{2,1,0:T(8,128)(2,1)}, u32[]{:S(2)}) copy-start(bf16[1,896,512]{2,1,0:T(8,128)(2,1)} %param.15) | copy-start | bytes 2752516
  101.2 3.8 %copy-start.2 = (s32[16]{0:T(128)S(1)}, s32[16]{0:T(128)}, u32[]{:S(2)}) copy-start(s32[16]{0:T(128)} %param.22) | copy-start | bytes 196
  101.2 29.1 %all-to-all-start.1 = ((bf16[1,16,56,512]{3,2,0,1:T(8,128)(2,1)}), bf16[1,16,56,512]{3,2,0,1:T(8,128)(2,1)S(1)}, u32[]{:S(2)}, u32[]{:S(2)}) async-start(bf16[1,16,56,512]{3,2,0,1:T(8,128)(2,1)} %bitcast.125), calls=%async_computation.2 | async-start | bytes 1835008 | tf_op jit(solution)/shard_map/all_to_all | solution.py:32
  131.9 6.1 %copy-start.3 = (bf16[1,896,512]{2,1,0:T(8,128)(2,1)S(1)}, bf16[1,896,512]{2,1,0:T(8,128)(2,1)}, u32[]{:S(2)}) copy-start(bf16[1,896,512]{2,1,0:T(8,128)(2,1)} %get-tuple-element.26) | copy-start | bytes 2752516
  134.2 31.3 %all-to-all-start.2 = ((bf16[1,16,56,512]{3,2,0,1:T(8,128)(2,1)}), bf16[1,16,56,512]{3,2,0,1:T(8,128)(2,1)S(1)}, u32[]{:S(2)}, u32[]{:S(2)}) async-start(bf16[1,16,56,512]{3,2,0,1:T(8,128)(2,1)} %fusion.26), calls=%async_computation.3 | async-start | bytes 1835008 | tf_op jit(solution)/shard_map/all_to_all | solution.py:34
  221.1 86.6 %all-to-all-start.3 = ((bf16[8,896,512]{2,1,0:T(8,128)(2,1)}), bf16[8,896,512]{2,1,0:T(8,128)(2,1)}, u32[]{:S(2)}, u32[]{:S(2)}) async-start(bf16[8,896,512]{2,1,0:T(8,128)(2,1)} %stack.46), calls=%async_computation.4 | async-start | bytes 14680064 | tf_op jit(solution)/shard_map/all_to_all | solution.py:104
  226.3 85.8 %all-gather.3.cloned.1.call-start = ((), (), s32[]{:S(2)}) async-start(), calls=%async_computation.8 | async-start | bytes 8552448 | tf_op jit(solution)/shard_map/all_gather | solution.py:95
  307.7 51.2 %all-to-all-start.5 = ((bf16[2,16,56,512]{3,2,0,1:T(8,128)(2,1)}), bf16[2,16,56,512]{3,2,0,1:T(8,128)(2,1)}, u32[]{:S(2)}, u32[]{:S(2)}) async-start(bf16[2,16,56,512]{3,2,0,1:T(8,128)(2,1)} %bitcast.121), calls=%async_computation.6 | async-start | bytes 3670016 | tf_op jit(solution)/shard_map/all_to_all | solution.py:34
  313.3 6.3 %copy-start.6 = (bf16[32,24,3712]{2,1,0:T(8,128)(2,1)S(1)}, bf16[32,24,3712]{2,1,0:T(8,128)(2,1)}, u32[]{:S(2)}) copy-start(bf16[32,24,3712]{2,1,0:T(8,128)(2,1)} %all-gather.3.cloned.1.call-done) | copy-start | bytes 17104900
  325.3 12.3 %collective-permute-start = (bf16[768,256]{1,0:T(8,128)(2,1)S(1)}, bf16[768,256]{1,0:T(8,128)(2,1)S(1)}, u32[]{:S(2)}, u32[]{:S(2)}) collective-permute-start(bf16[768,256]{1,0:T(8,128)(2,1)S(1)} %get-tuple-element.30), channel_id=1, source_target_pairs={{0,1},{1,0},{2,3},{3,2},{4,5},{5,4},{6,7},{7,6},{8,9},{9,8},{10,11... | collective-permute-start | bytes 1179656 | tf_op jit(solution)/shard_map/ppermute | solution.py:121
  361.9 2.4 copy-start.1
Sparse Core Ops, SparseCore 0:
  12.3 45.8 reduce-scatter.1
  228.9 73.1 all-gather.2
